TPU v7x, 128 devices: a whole 4x4x4 slice. The times are simulated.
128 devices in a mesh: tm: 32 (over x, z, core), feat: 4 (over y).
Axes of the slice: x: 4, y: 4, z: 4, core: 2. Of those that a mesh axis runs over, the one named last changes fastest.
Arguments:
- activations: bfloat16 [81920, 2048], P(('tm', 'feat')), may hold values from -19 to 19
- targets: bfloat16 [81920, 128], P(('tm', 'feat')), may hold values from -8 to 8
- span_of: int32 [81920], P(('tm', 'feat')), may hold values from 0 to 31, as said below
Outputs:
- predictions: bfloat16 [81920, 128], P(('tm', 'feat'))
- surprise: float32 [81920], P(('tm', 'feat'))
Inputs may be any that keep to these rules, and one draw needn't show every extreme that they name: `span_of`: in each aligned block of 640 rows (the rows of one device) every span from 0 to 31 appears exactly 20 times.
All inputs are finite; a program needn't handle non-finite values.
Results may differ from a plain program's by a relative error of at most 0.0049.
Values may be sent and summed in bfloat16 or wider, within the bound.
No kernel may reach another device: no remote copies, remote signals or barrier semaphores. Data moves between devices by JAX's collectives and lax.ppermute only.
A program may use at most 320 MiB of HBM per device.

v0:
```python
import jax
import jax.numpy as jnp
from jax import lax
from jax.sharding import Mesh, PartitionSpec as P

ITERS = 3
RIDGE = 0.1
TINY = 1e-06
TM = ("x", "z", "c")
SWAP = [(0, 1), (1, 0)]


def masked_sum(stack, position):
    keep = jnp.arange(stack.shape[0]) < position
    return jnp.sum(jnp.where(keep.reshape((-1,) + (1,) * (stack.ndim - 1)), stack, 0.0), axis=0)


def exclusive_prefix(block):
    ci = lax.axis_index("c")
    zi = lax.axis_index("z")
    xi = lax.axis_index("x")
    rows = block.shape[0]
    half = rows // 2
    partner = lax.ppermute(block, "c", SWAP)
    chip = block + partner
    below = jnp.where(ci == 1, partner, 0.0)
    mine = lax.dynamic_slice_in_dim(chip, ci * half, half, 0)
    along_z = lax.all_gather(mine, "z")
    before_z = masked_sum(along_z, zi)
    total_z = jnp.sum(along_z, axis=0)
    along_x = lax.all_gather(total_z, "x")
    before_x = masked_sum(along_x, xi)
    mine_prefix = before_x + before_z
    other_prefix = lax.ppermute(mine_prefix, "c", SWAP)
    joined = jnp.zeros((rows,) + block.shape[1:], block.dtype)
    joined = lax.dynamic_update_slice_in_dim(joined, mine_prefix, ci * half, 0)
    joined = lax.dynamic_update_slice_in_dim(joined, other_prefix, (1 - ci) * half, 0)
    return joined + below


def body(activations, targets, span_of):
    spans = lax.axis_size(TM)
    feat_count = lax.axis_size("feat")
    tok_dev, width = activations.shape
    n_targets = targets.shape[1]
    block_rows = width // feat_count
    share = tok_dev // spans
    contract = (((0,), (0,)), ((), ()))
    highest = lax.Precision.HIGHEST
    order = jnp.argsort(span_of, stable=True)
    sorted_x = jnp.take(activations, order, axis=0).reshape(spans, share, width)
    sorted_y = jnp.take(targets, order, axis=0).reshape(spans, share, n_targets)
    moved_x, moved_y = (
        lax.all_to_all(sorted_x, TM, split_axis=0, concat_axis=0, tiled=True),
        lax.all_to_all(sorted_y, TM, split_axis=0, concat_axis=0, tiled=True),
    )
    local_x = moved_x.reshape(tok_dev, width)
    local_y = moved_y.reshape(tok_dev, n_targets)
    col_start = lax.axis_index("feat") * block_rows
    rows_x = lax.all_gather(local_x, "feat", axis=0, tiled=True)
    rows_y = lax.all_gather(local_y, "feat", axis=0, tiled=True)
    own = lax.dynamic_slice_in_dim(rows_x, col_start, block_rows, 1)
    gram_part = lax.dot_general(own, rows_x, contract, preferred_element_type=jnp.float32)
    cross_part = lax.dot_general(own, rows_y, contract, preferred_element_type=jnp.float32)
    gram_prefix = exclusive_prefix(gram_part)
    cross_prefix = exclusive_prefix(cross_part)
    span = (lax.axis_index("x") * lax.axis_size("z") + lax.axis_index("z")) * lax.axis_size(
        "c"
    ) + lax.axis_index("c")
    seen = (span * (tok_dev * feat_count)).astype(jnp.float32)
    scale = 1.0 / jnp.maximum(seen, 1.0)
    rhs = scale * cross_prefix

    def column_dot(left, right):
        return lax.psum(jnp.sum(left * right, axis=0), "feat")

    residual = rhs
    direction = rhs
    norm_now = column_dot(residual, residual)
    solution = None
    for step in range(ITERS):
        product = jnp.dot(
            gram_prefix,
            lax.all_gather(direction, "feat", axis=0, tiled=True),
            precision=highest,
            preferred_element_type=jnp.float32,
        )
        image = scale * product + RIDGE * direction
        alpha = norm_now / (column_dot(direction, image) + TINY)
        update = alpha * direction
        solution = update if solution is None else solution + update
        if step + 1 < ITERS:
            residual = residual - alpha * image
            norm_next = column_dot(residual, residual)
            direction = residual + norm_next / (norm_now + TINY) * direction
            norm_now = norm_next
    weights = lax.all_gather(solution.astype(jnp.bfloat16), "feat", axis=0, tiled=True)
    predicted = jnp.dot(local_x, weights, preferred_element_type=jnp.float32).astype(jnp.bfloat16)
    returned = lax.all_to_all(
        predicted.reshape(spans, share, n_targets), TM, split_axis=0, concat_axis=0, tiled=True
    )
    in_order = returned.reshape(tok_dev, n_targets)
    predictions = jnp.zeros_like(in_order).at[order].set(in_order)
    error = targets.astype(jnp.float32) - predictions.astype(jnp.float32)
    surprise = jnp.mean(error * error, axis=1)
    return (predictions, surprise)


def solution(mesh):
    tm = mesh.shape["tm"]
    feat = mesh.shape["feat"]
    fine = Mesh(mesh.devices.reshape(tm // 8, 4, 2, feat), TM + ("feat",))
    rows = TM + ("feat",)
    return jax.shard_map(
        body,
        mesh=fine,
        in_specs=(P(rows, None), P(rows, None), P(rows)),
        out_specs=(P(rows, None), P(rows)),
        check_vma=False,
    )
```

profile of v0, /device:TPU:1, one launch (start us, length us, event | category | flops | bytes accessed | tf_op | source)
XLA Modules:
  0.0 592.7 jit_solution(11710074773149398378)
XLA Ops:
  7.2 0.0 all-gather.11.cloned.1.call-start
  7.2 5.2 sort.17
  12.5 4.1 gather_fusion
  16.6 5.2 gather.13
  21.7 0.1 broadcast_in_dim.83
  21.9 2.2 broadcast_select_fusion
  24.1 48.7 %all_to_all.15 = bf16[32,20,2048]{2,1,0:T(8,128)(2,1)} all-to-all(bf16[32,20,2048]{2,1,0:T(8,128)(2,1)S(1)} %broadcast_select_fusion), channel_id=1, replica_groups=mesh['x'=4,'z'=4,'c'=2,'feat'=4] {'x','z','c'}, dimensions={0} | all-to-all | bytes 5242880 | tf_op jit(solution)/shard_map/all_to_all | solution.py:54
  72.8 5.2 reshape.51
  78.0 0.0 all-gather.11.cloned.1.call-update
  78.0 0.0 all-gather.19.cloned.1.call-start
  78.1 98.4 %all-gather.11.cloned.1.call-done = bf16[2560,2048]{1,0:T(8,128)(2,1)} async-done(((bf16[640,2048]{1,0:T(8,128)(2,1)}), bf16[2560,2048]{1,0:T(8,128)(2,1)}) %all-gather.11.cloned.1.call-update) | async-done | bytes 10485776 | tf_op jit(solution)/shard_map/all_gather | solution.py:60
  176.5 10.4 %fusion = f32[512,2048]{1,0:T(8,128)} fusion(bf16[2560,2048]{1,0:T(8,128)(2,1)} %all-gather.11.cloned.1.call-done, s32[]{:T(128)S(6)} %select_n.63), kind=kOutput, calls=%fused_computation.7 | convolution fusion | flops 5368709120 | bytes 17301508 | tf_op jit(solution)/shard_map/dot_general | solution.py:63
  186.9 0.8 collective-permute-start.2
  187.8 7.1 %collective-permute-done.2 = f32[512,2048]{1,0:T(8,128)} collective-permute-done((f32[512,2048]{1,0:T(8,128)}, f32[512,2048]{1,0:T(8,128)}, u32[]{:S(2)}, u32[]{:S(2)}) %collective-permute-start.2) | collective-permute-done | bytes 4194336 | tf_op jit(solution)/shard_map/ppermute | solution.py:24
  194.9 3.9 dynamic-slice_add_fusion
  198.9 0.0 all-gather.21.cloned.1.call-start
  198.9 83.9 %all-gather.19.cloned.1.call-done = f32[1024,2048]{1,0:T(8,128)} async-done(((f32[256,2048]{1,0:T(8,128)}), f32[1024,2048]{1,0:T(8,128)}) %all-gather.19.cloned.1.call-update) | async-done | bytes 8388624 | tf_op jit(solution)/shard_map/all_gather | solution.py:28
  282.8 6.5 %select_reduce_fusion = (f32[256,2048]{1,0:T(8,128)S(1)}, f32[256,2048]{1,0:T(8,128)}) fusion(f32[4,256,2048]{2,1,0:T(8,128)} %bitcast.14, pred[4]{0:T(512)(128)(4,1)S(1)} %iota_compare_fusion), kind=kLoop, calls=%fused_computation.3 | loop fusion | flops 5242880 | bytes 12582916 | tf_op jit(solution)/shard_map/reduce_sum | solution.py:15
  289.4 2.0 gather_fusion.1
  291.4 0.9 broadcast_select_fusion.1
  292.3 7.4 %all-to-all-start.1 = ((bf16[32,20,128]{2,1,0:T(8,128)(2,1)}), bf16[32,20,128]{2,1,0:T(8,128)(2,1)S(1)}, u32[]{:S(2)}, u32[]{:S(2)}) async-start(bf16[32,20,128]{2,1,0:T(8,128)(2,1)} %broadcast_select_fusion.1), calls=%async_computation.1 | async-start | bytes 393216 | tf_op jit(solution)/shard_map/all_to_all | solution.py:55
  299.7 0.0 all-gather.13.cloned.1.call-start
  299.7 8.2 %all-to-all-done.1 = bf16[32,20,128]{2,1,0:T(8,128)(2,1)S(1)} async-done(((bf16[32,20,128]{2,1,0:T(8,128)(2,1)}), bf16[32,20,128]{2,1,0:T(8,128)(2,1)S(1)}, u32[]{:S(2)}, u32[]{:S(2)}) %all-to-all-start.1) | async-done | bytes 163872 | tf_op jit(solution)/shard_map/all_to_all | solution.py:55
  308.0 11.8 %all_gather.43 = bf16[2560,128]{1,0:T(8,128)(2,1)S(1)} all-gather(bf16[640,128]{1,0:T(8,128)(2,1)S(1)} %reshape.52), channel_id=1, replica_groups=mesh['x'=4,'z'=4,'c'=2,'feat'=4] {'feat'}, dimensions={0}, use_global_device_ids=true | all-gather | bytes 819200 | tf_op jit(solution)/shard_map/all_gather | solution.py:61
  319.8 2.6 fusion.2
  322.4 2.1 collective-permute-start
  324.5 48.8 %all-gather.21.cloned.1.call-done = f32[1024,2048]{1,0:T(8,128)} async-done(((f32[256,2048]{1,0:T(8,128)}), f32[1024,2048]{1,0:T(8,128)}) %all-gather.21.cloned.1.call-update) | async-done | bytes 8388624 | tf_op jit(solution)/shard_map/all_gather | solution.py:31
  373.4 4.7 select_reduce_fusion.1
  378.1 2.5 broadcast_in_dim.92
  380.6 2.5 constant_dynamic-update-slice_fusion.1
  383.1 0.8 collective-permute-start.3
  383.9 11.2 %all-gather = f32[1024,128]{1,0:T(8,128)S(1)} all-gather(f32[256,128]{1,0:T(8,128)S(1)} %dynamic-slice_add_fusion.1), channel_id=2, replica_groups=mesh['x'=4,'z'=4,'c'=2,'feat'=4] {'z'}, dimensions={0}, use_global_device_ids=true | all-gather | bytes 655360 | tf_op jit(solution)/shard_map/all_gather | solution.py:28
  395.1 0.1 select_reduce_fusion.2
  395.2 10.4 %all-gather.1 = f32[1024,128]{1,0:T(8,128)S(1)} all-gather(f32[256,128]{1,0:T(8,128)S(1)} %get-tuple-element.7), channel_id=3, replica_groups=mesh['x'=4,'z'=4,'c'=2,'feat'=4] {'x'}, dimensions={0}, use_global_device_ids=true | all-gather | bytes 655360 | tf_op jit(solution)/shard_map/all_gather | solution.py:31
  405.6 0.1 select_reduce_fusion.3
  405.7 5.3 collective-permute-start.1
  411.1 0.9 collective-permute-done.1
  412.1 0.7 add_multiply_fusion
  412.8 0.0 all-gather.15.cloned.1.call-start
  412.9 1.6 constant_dynamic-update-slice_fusion
  414.4 6.6 %select_add_fusion = f32[512,2048]{1,0:T(8,128)} fusion(f32[512,2048]{1,0:T(8,128)} %constant_dynamic-update-slice_fusion, f32[512,2048]{1,0:T(8,128)} %collective-permute-done.2, pred[]{:T(512)S(6)} %eq.4), kind=kLoop, calls=%fused_computation.5 | loop fusion | flops 2097152 | bytes 12582913 | tf_op jit(solution)/shard_map/add | solution.py:38
  421.1 13.0 %all-gather.13.cloned.1.call-done = f32[2048,128]{1,0:T(8,128)} async-done(((f32[512,128]{1,0:T(8,128)}), f32[2048,128]{1,0:T(8,128)}) %all-gather.13.cloned.1.call-update) | async-done | bytes 1048592 | tf_op jit(solution)/shard_map/all_gather | solution.py:84
  434.1 5.5 multiply_reduce_fusion.4
  439.6 7.7 %all-reduce = (f32[128]{0:T(128)S(1)}, f32[128]{0:T(128)S(1)}) all-reduce(f32[128]{0:T(128)S(1)} %get-tuple-element.9, f32[128]{0:T(128)S(1)} %get-tuple-element.8), channel_id=1, replica_groups=mesh['x'=4,'z'=4,'c'=2,'feat'=4] {'feat'}, use_global_device_ids=true, to_apply=%region_5.6 | all-reduce | flops 256 | bytes 2048 | tf_op jit(solution)/shard_map/psum | solution.py:75
  447.3 0.1 multiply_reduce_fusion.3
  447.4 6.0 %psum.44 = f32[128]{0:T(128)S(1)} all-reduce(f32[128]{0:T(128)S(1)} %get-tuple-element.12), channel_id=1, replica_groups=mesh['x'=4,'z'=4,'c'=2,'feat'=4] {'feat'}, use_global_device_ids=true, to_apply=%region_12.13 | all-reduce | flops 128 | bytes 1024 | tf_op jit(solution)/shard_map/psum | solution.py:75
  453.4 0.7 multiply_add_fusion.1
  454.2 0.0 all-gather.17.cloned.1.call-start
  454.2 27.8 %all-gather.15.cloned.1.call-done = f32[2048,128]{1,0:T(8,128)} async-done(((f32[512,128]{1,0:T(8,128)}), f32[2048,128]{1,0:T(8,128)}) %all-gather.15.cloned.1.call-update) | async-done | bytes 1048592 | tf_op jit(solution)/shard_map/all_gather | solution.py:84
  482.0 5.9 %multiply_reduce_fusion.2 = (f32[128]{0:T(128)S(1)}, f32[512,128]{1,0:T(8,128)S(1)}) fusion(f32[512,128]{1,0:T(8,128)} %multiply_add_fusion.1, f32[512,2048]{1,0:T(8,128)} %select_add_fusion, f32[2048,128]{1,0:T(8,128)} %all-gather.15.cloned.1.call-done, f32[]{:T(128)S(6)} %div.24), kind=kOutput, calls=%fused_computation.28 | convolution fusion | flops 1610940288 | bytes 5767684 | tf_op jit(solution)/shard_map/dot_general | solution.py:82
  488.0 7.7 %psum.45 = f32[128]{0:T(128)S(1)} all-reduce(f32[128]{0:T(128)S(1)} %get-tuple-element.19), channel_id=1, replica_groups=mesh['x'=4,'z'=4,'c'=2,'feat'=4] {'feat'}, use_global_device_ids=true, to_apply=%region_14.15 | all-reduce | flops 128 | bytes 1024 | tf_op jit(solution)/shard_map/psum | solution.py:75
  495.7 0.1 multiply_reduce_fusion.1
  495.8 6.0 %psum.46 = f32[128]{0:T(128)S(1)} all-reduce(f32[128]{0:T(128)S(1)} %multiply_reduce_fusion.1), channel_id=1, replica_groups=mesh['x'=4,'z'=4,'c'=2,'feat'=4] {'feat'}, use_global_device_ids=true, to_apply=%region_16.17 | all-reduce | flops 128 | bytes 1024 | tf_op jit(solution)/shard_map/psum | solution.py:75
  501.8 0.8 multiply_add_fusion
  502.6 27.8 %all-gather.17.cloned.1.call-done = f32[2048,128]{1,0:T(8,128)} async-done(((f32[512,128]{1,0:T(8,128)}), f32[2048,128]{1,0:T(8,128)}) %all-gather.17.cloned.1.call-update) | async-done | bytes 1048592 | tf_op jit(solution)/shard_map/all_gather | solution.py:84
  530.4 6.1 %fusion.8 = f32[128]{0:T(128)S(1)} fusion(f32[512,128]{1,0:T(8,128)} %multiply_add_fusion, f32[512,2048]{1,0:T(8,128)} %select_add_fusion, f32[2048,128]{1,0:T(8,128)} %all-gather.17.cloned.1.call-done, f32[]{:T(128)S(6)} %div.24), kind=kOutput, calls=%fused_computation.20 | convolution fusion | flops 1610940288 | bytes 5505540 | tf_op jit(solution)/shard_map/dot_general | solution.py:82
  536.5 7.7 %psum.47 = f32[128]{0:T(128)S(1)} all-reduce(f32[128]{0:T(128)S(1)} %fusion.8), channel_id=1, replica_groups=mesh['x'=4,'z'=4,'c'=2,'feat'=4] {'feat'}, use_global_device_ids=true, to_apply=%region_18.19 | all-reduce | flops 128 | bytes 1024 | tf_op jit(solution)/shard_map/psum | solution.py:75
  544.2 1.0 add_convert_fusion
  545.2 10.8 %all_gather.55 = bf16[2048,128]{1,0:T(8,128)(2,1)S(1)} all-gather(bf16[512,128]{1,0:T(8,128)(2,1)S(1)} %add_convert_fusion), channel_id=1, replica_groups=mesh['x'=4,'z'=4,'c'=2,'feat'=4] {'feat'}, dimensions={0}, use_global_device_ids=true | all-gather | bytes 655360 | tf_op jit(solution)/shard_map/all_gather | solution.py:97
  556.0 2.6 convolution_convert_fusion
  558.6 22.2 %all_to_all.16 = bf16[32,20,128]{2,1,0:T(8,128)(2,1)S(1)} all-to-all(bf16[32,20,128]{2,1,0:T(8,128)(2,1)S(1)} %reshape.53), channel_id=1, replica_groups=mesh['x'=4,'z'=4,'c'=2,'feat'=4] {'x','z','c'}, dimensions={0} | all-to-all | bytes 327680 | tf_op jit(solution)/shard_map/all_to_all | solution.py:99
  580.8 4.3 scatter_custom_fusion
  585.1 0.2 multiply_reduce_fusion
  585.3 0.6 broadcast_multiply_fusion
  (38 shorter events, 0.4 us)
Async XLA Ops:
  7.2 5.3 copy-start
  7.2 169.3 %all-gather.11.cloned.1.call-start = ((), (), s32[]{:S(2)}) async-start(), calls=%async_computation.3 | async-start | bytes 13107200 | tf_op jit(solution)/shard_map/all_gather | solution.py:60
  78.0 204.8 %all-gather.19.cloned.1.call-start = ((), (), s32[]{:S(2)}) async-start(), calls=%async_computation.7 | async-start | bytes 10485760 | tf_op jit(solution)/shard_map/all_gather | solution.py:28
  186.9 8.0 %collective-permute-start.2 = (f32[512,2048]{1,0:T(8,128)}, f32[512,2048]{1,0:T(8,128)}, u32[]{:S(2)}, u32[]{:S(2)}) collective-permute-start(f32[512,2048]{1,0:T(8,128)} %fusion), channel_id=1, source_target_pairs={{0,4},{4,0},{1,5},{5,1},{2,6},{6,2},{3,7},{7,3},{8,12},{12,8},{9,1... | collective-permute-start | bytes 12582920 | tf_op jit(solution)/shard_map/ppermute | solution.py:24
  198.9 174.5 %all-gather.21.cloned.1.call-start = ((), (), s32[]{:S(2)}) async-start(), calls=%async_computation.8 | async-start | bytes 10485760 | tf_op jit(solution)/shard_map/all_gather | solution.py:31
  282.8 6.6 %copy-start.2 = (bf16[640,128]{1,0:T(8,128)(2,1)S(1)}, bf16[640,128]{1,0:T(8,128)(2,1)}, u32[]{:S(2)}) copy-start(bf16[640,128]{1,0:T(8,128)(2,1)} %param.4) | copy-start | bytes 491524
  292.3 15.7 %all-to-all-start.1 = ((bf16[32,20,128]{2,1,0:T(8,128)(2,1)}), bf16[32,20,128]{2,1,0:T(8,128)(2,1)S(1)}, u32[]{:S(2)}, u32[]{:S(2)}) async-start(bf16[32,20,128]{2,1,0:T(8,128)(2,1)} %broadcast_select_fusion.1), calls=%async_computation.1 | async-start | bytes 393216 | tf_op jit(solution)/shard_map/all_to_all | solution.py:55
  299.7 134.4 %all-gather.13.cloned.1.call-start = ((), (), s32[]{:S(2)}) async-start(), calls=%async_computation.4 | async-start | bytes 1310720 | tf_op jit(solution)/shard_map/all_gather | solution.py:84
  322.4 61.4 %collective-permute-start = (f32[512,128]{1,0:T(8,128)S(1)}, f32[512,128]{1,0:T(8,128)S(1)}, u32[]{:S(2)}, u32[]{:S(2)}) collective-permute-start(f32[512,128]{1,0:T(8,128)S(1)} %fusion.2), channel_id=1, source_target_pairs={{0,4},{4,0},{1,5},{5,1},{2,6},{6,2},{3,7},{7,3},{8,12},{12,8},{9,1... | collective-permute-start | bytes 786440 | tf_op jit(solution)/shard_map/ppermute | solution.py:24
  383.1 29.8 %collective-permute-start.3 = (f32[256,2048]{1,0:T(8,128)}, f32[256,2048]{1,0:T(8,128)S(1)}, u32[]{:S(2)}, u32[]{:S(2)}) collective-permute-start(f32[256,2048]{1,0:T(8,128)} %get-tuple-element.15), channel_id=1, source_target_pairs={{0,4},{4,0},{1,5},{5,1},{2,6},{6,2},{3,7},{7,3},{8,12},{12,8},{9,1... | collective-permute-start | bytes 6291464 | tf_op jit(solution)/shard_map/ppermute | solution.py:34
  405.7 6.3 %collective-permute-start.1 = (f32[256,128]{1,0:T(8,128)S(1)}, f32[256,128]{1,0:T(8,128)S(1)}, u32[]{:S(2)}, u32[]{:S(2)}) collective-permute-start(f32[256,128]{1,0:T(8,128)S(1)} %get-tuple-element.17), channel_id=1, source_target_pairs={{0,4},{4,0},{1,5},{5,1},{2,6},{6,2},{3,7},{7,3},{8,12},{12,8},{9,1... | collective-permute-start | bytes 393224 | tf_op jit(solution)/shard_map/ppermute | solution.py:34
  412.8 69.2 %all-gather.15.cloned.1.call-start = ((), (), s32[]{:S(2)}) async-start(), calls=%async_computation.5 | async-start | bytes 1310720 | tf_op jit(solution)/shard_map/all_gather | solution.py:84
  414.4 19.7 %copy-start.3 = (f32[512,128]{1,0:T(8,128)S(1)}, f32[512,128]{1,0:T(8,128)}, u32[]{:S(2)}) copy-start(f32[512,128]{1,0:T(8,128)} %add_multiply_fusion) | copy-start | bytes 786436
  454.2 47.6 %copy-start.4 = (f32[512,128]{1,0:T(8,128)S(1)}, f32[512,128]{1,0:T(8,128)}, u32[]{:S(2)}) copy-start(f32[512,128]{1,0:T(8,128)} %multiply_add_fusion.1) | copy-start | bytes 786436
  454.2 76.2 %all-gather.17.cloned.1.call-start = ((), (), s32[]{:S(2)}) async-start(), calls=%async_computation.6 | async-start | bytes 1310720 | tf_op jit(solution)/shard_map/all_gather | solution.py:84
  530.4 55.5 %copy-start.1 = (bf16[640,2048]{1,0:T(8,128)(2,1)S(1)}, bf16[640,2048]{1,0:T(8,128)(2,1)}, u32[]{:S(2)}) copy-start(bf16[640,2048]{1,0:T(8,128)(2,1)} %param.3) | copy-start | bytes 7864324
  585.1 0.8 copy-start.5
Sparse Core Ops, SparseCore 0:
  78.1 98.3 all-gather.10
  199.0 83.7 all-gather.18
  289.5 83.8 all-gather.20
  412.9 21.1 all-gather.12
  454.3 27.6 all-gather.14
  502.7 27.6 all-gather.16
where the time goes:
time: 594 us; the launch traced here: 593 us
  waiting for transfers between devices  316 us (53%)
  blocking collectives  150 us (25%)
  other arithmetic  37.2 us (6%)
  matrix products  33.2 us (6%)
  local copies, waits for them, and re-layouts  25.1 us (4%)
  starting transfers between devices  16.6 us (3%)
  between operations  14.4 us (2%)
    all_gather x1, waiting for transfers between devices, body(): rows_x = lax.all_gather(local_x, 'feat', axis=0, tiled=True)  98.4 us
    all_gather x1, waiting for transfers between devices, exclusive_prefix(): along_z = lax.all_gather(mine, 'z')  83.9 us
    all_gather x3, waiting for transfers between devices, body(): lax.all_gather(direction, 'feat', axis=0, tiled=True)  68.6 us
    all_gather x1, waiting for transfers between devices, exclusive_prefix(): along_x = lax.all_gather(total_z, 'x')  48.8 us
    all_to_all x1, blocking collectives, body(): lax.all_to_all(sorted_x, TM, split_axis=0, concat_axis=0, tiled=True)  48.7 us
    psum x5, blocking collectives, column_dot(): return lax.psum(jnp.sum(left * right, axis=0), 'feat')  35.1 us
    all_to_all x1, blocking collectives, body(): lax.all_to_all(predicted.reshape(spans, share, n_targets), TM, split_axis...  22.2 us
    dot_general x3, matrix products, body(): jnp.dot(gram_prefix, lax.all_gather(direction, 'feat', axis=0, tiled=True...  17.6 us
  transfers between devices with their start and end apart: 11, of which 9 were waited for; matrix products, arithmetic and copies ran while one was open for 4% of the time, Pallas kernels for 0%

commit v1 on v0

--- a/solution.py
+++ b/solution.py
@@ -57,7 +57,9 @@
     local_x = moved_x.reshape(tok_dev, width)
     local_y = moved_y.reshape(tok_dev, n_targets)
     col_start = lax.axis_index("feat") * block_rows
-    rows_x = lax.all_gather(local_x, "feat", axis=0, tiled=True)
+    rows_x = jnp.concatenate(
+        lax.all_to_all(jnp.stack([local_x] * lax.axis_size("feat")), "feat", 0, 0), axis=0
+    )
     rows_y = lax.all_gather(local_y, "feat", axis=0, tiled=True)
     own = lax.dynamic_slice_in_dim(rows_x, col_start, block_rows, 1)
     gram_part = lax.dot_general(own, rows_x, contract, preferred_element_type=jnp.float32)

time: 594 us -> 617 us (1.039)
  waiting for transfers between devices: 316 us -> 328 us
  starting transfers between devices: 16.6 us -> 22.9 us
    all_to_all x0 -> x1, waiting for transfers between devices: none -> 116 us  [body(): lax.all_to_all(jnp.stack([local_x] * lax.axis_size('feat')), 'feat', 0, 0)]
    all_gather x1 -> x0, waiting for transfers between devices: 98.4 us -> none  [body(): rows_x = lax.all_gather(local_x, 'feat', axis=0, tiled=True)]
where the time goes in v1:
time: 617 us; the launch traced here: 616 us
  waiting for transfers between devices  328 us (53%)
  blocking collectives  150 us (24%)
  other arithmetic  37.2 us (6%)
  matrix products  33.2 us (5%)
  local copies, waits for them, and re-layouts  28.8 us (5%)
  starting transfers between devices  22.9 us (4%)
  between operations  16 us (3%)
    all_to_all x1, waiting for transfers between devices, body(): lax.all_to_all(jnp.stack([local_x] * lax.axis_size('feat')), 'feat', 0, 0)  116 us
    all_gather x1, waiting for transfers between devices, exclusive_prefix(): along_z = lax.all_gather(mine, 'z')  78.8 us
    all_gather x3, waiting for transfers between devices, body(): lax.all_gather(direction, 'feat', axis=0, tiled=True)  68.2 us
    all_to_all x1, blocking collectives, body(): lax.all_to_all(sorted_x, TM, split_axis=0, concat_axis=0, tiled=True)  48.7 us
    all_gather x1, waiting for transfers between devices, exclusive_prefix(): along_x = lax.all_gather(total_z, 'x')  48.7 us
    psum x5, blocking collectives, column_dot(): return lax.psum(jnp.sum(left * right, axis=0), 'feat')  35.4 us
    all_to_all x1, blocking collectives, body(): lax.all_to_all(predicted.reshape(spans, share, n_targets), TM, split_axis...  22.1 us
    dot_general x3, matrix products, body(): jnp.dot(gram_prefix, lax.all_gather(direction, 'feat', axis=0, tiled=True...  17.6 us
  transfers between devices with their start and end apart: 11, of which 9 were waited for; matrix products, arithmetic and copies ran while one was open for 4% of the time, Pallas kernels for 0%

profile of v1, /device:TPU:1, one launch (start us, length us, event | category | flops | bytes accessed | tf_op | source)
XLA Modules:
  0.0 616.4 jit_solution(5379185059910112236)
XLA Ops:
  8.0 5.2 sort.17
  13.3 4.1 gather_fusion
  17.4 5.2 gather.13
  22.5 0.1 broadcast_in_dim.83
  22.6 2.2 broadcast_select_fusion
  24.9 48.7 %all_to_all.20 = bf16[32,20,2048]{2,1,0:T(8,128)(2,1)} all-to-all(bf16[32,20,2048]{2,1,0:T(8,128)(2,1)S(1)} %broadcast_select_fusion), channel_id=1, replica_groups=mesh['x'=4,'z'=4,'c'=2,'feat'=4] {'x','z','c'}, dimensions={0} | all-to-all | bytes 5242880 | tf_op jit(solution)/shard_map/all_to_all | solution.py:54
  73.6 3.6 reshape.56
  77.3 5.3 stack.3
  82.5 6.0 all-to-all-start.1
  88.5 0.0 all-gather.16.cloned.1.call-start
  88.6 116.2 %all-to-all-done.1 = bf16[4,640,2048]{2,1,0:T(8,128)(2,1)} async-done(((bf16[4,640,2048]{2,1,0:T(8,128)(2,1)}), bf16[4,640,2048]{2,1,0:T(8,128)(2,1)}, u32[]{:S(2)}, u32[]{:S(2)}) %all-to-all-start.1) | async-done | bytes 10485792 | tf_op jit(solution)/shard_map/all_to_all | solution.py:61
  204.8 10.4 %fusion = f32[512,2048]{1,0:T(8,128)} fusion(bf16[2560,2048]{1,0:T(8,128)(2,1)} %bitcast, s32[]{:T(128)S(6)} %select_n.63), kind=kOutput, calls=%fused_computation.7 | convolution fusion | flops 5368709120 | bytes 17301508 | tf_op jit(solution)/shard_map/dot_general | solution.py:65
  215.2 1.0 collective-permute-start.2
  216.2 7.1 %collective-permute-done.2 = f32[512,2048]{1,0:T(8,128)} collective-permute-done((f32[512,2048]{1,0:T(8,128)}, f32[512,2048]{1,0:T(8,128)}, u32[]{:S(2)}, u32[]{:S(2)}) %collective-permute-start.2) | collective-permute-done | bytes 4194336 | tf_op jit(solution)/shard_map/ppermute | solution.py:24
  223.3 3.9 dynamic-slice_add_fusion
  227.2 0.0 all-gather.18.cloned.1.call-start
  227.3 78.8 %all-gather.16.cloned.1.call-done = f32[1024,2048]{1,0:T(8,128)} async-done(((f32[256,2048]{1,0:T(8,128)}), f32[1024,2048]{1,0:T(8,128)}) %all-gather.16.cloned.1.call-update) | async-done | bytes 8388624 | tf_op jit(solution)/shard_map/all_gather | solution.py:28
  306.1 6.5 %select_reduce_fusion = (f32[256,2048]{1,0:T(8,128)S(1)}, f32[256,2048]{1,0:T(8,128)}) fusion(f32[4,256,2048]{2,1,0:T(8,128)} %bitcast.15, pred[4]{0:T(512)(128)(4,1)S(1)} %iota_compare_fusion), kind=kLoop, calls=%fused_computation.3 | loop fusion | flops 5242880 | bytes 12582916 | tf_op jit(solution)/shard_map/reduce_sum | solution.py:15
  312.7 2.0 gather_fusion.1
  314.7 0.9 broadcast_select_fusion.1
  315.6 7.4 %all-to-all-start.2 = ((bf16[32,20,128]{2,1,0:T(8,128)(2,1)}), bf16[32,20,128]{2,1,0:T(8,128)(2,1)S(1)}, u32[]{:S(2)}, u32[]{:S(2)}) async-start(bf16[32,20,128]{2,1,0:T(8,128)(2,1)} %broadcast_select_fusion.1), calls=%async_computation.2 | async-start | bytes 393216 | tf_op jit(solution)/shard_map/all_to_all | solution.py:55
  323.0 0.0 all-gather.10.cloned.1.call-start
  323.1 8.2 %all-to-all-done.2 = bf16[32,20,128]{2,1,0:T(8,128)(2,1)S(1)} async-done(((bf16[32,20,128]{2,1,0:T(8,128)(2,1)}), bf16[32,20,128]{2,1,0:T(8,128)(2,1)S(1)}, u32[]{:S(2)}, u32[]{:S(2)}) %all-to-all-start.2) | async-done | bytes 163872 | tf_op jit(solution)/shard_map/all_to_all | solution.py:55
  331.3 11.8 %all_gather.39 = bf16[2560,128]{1,0:T(8,128)(2,1)S(1)} all-gather(bf16[640,128]{1,0:T(8,128)(2,1)S(1)} %reshape.58), channel_id=1, replica_groups=mesh['x'=4,'z'=4,'c'=2,'feat'=4] {'feat'}, dimensions={0}, use_global_device_ids=true | all-gather | bytes 819200 | tf_op jit(solution)/shard_map/all_gather | solution.py:63
  343.1 2.6 fusion.2
  345.8 2.2 collective-permute-start
  348.0 48.7 %all-gather.18.cloned.1.call-done = f32[1024,2048]{1,0:T(8,128)} async-done(((f32[256,2048]{1,0:T(8,128)}), f32[1024,2048]{1,0:T(8,128)}) %all-gather.18.cloned.1.call-update) | async-done | bytes 8388624 | tf_op jit(solution)/shard_map/all_gather | solution.py:31
  396.7 4.7 select_reduce_fusion.1
  401.4 2.5 broadcast_in_dim.92
  403.9 2.5 constant_dynamic-update-slice_fusion.1
  406.4 0.8 collective-permute-start.3
  407.2 11.2 %all-gather = f32[1024,128]{1,0:T(8,128)S(1)} all-gather(f32[256,128]{1,0:T(8,128)S(1)} %dynamic-slice_add_fusion.1), channel_id=2, replica_groups=mesh['x'=4,'z'=4,'c'=2,'feat'=4] {'z'}, dimensions={0}, use_global_device_ids=true | all-gather | bytes 655360 | tf_op jit(solution)/shard_map/all_gather | solution.py:28
  418.4 0.1 select_reduce_fusion.2
  418.5 10.4 %all-gather.1 = f32[1024,128]{1,0:T(8,128)S(1)} all-gather(f32[256,128]{1,0:T(8,128)S(1)} %get-tuple-element.7), channel_id=3, replica_groups=mesh['x'=4,'z'=4,'c'=2,'feat'=4] {'x'}, dimensions={0}, use_global_device_ids=true | all-gather | bytes 655360 | tf_op jit(solution)/shard_map/all_gather | solution.py:31
  428.9 0.1 select_reduce_fusion.3
  429.1 5.3 collective-permute-start.1
  434.4 0.9 collective-permute-done.1
  435.4 0.7 add_multiply_fusion
  436.1 0.0 all-gather.12.cloned.1.call-start
  436.2 1.6 constant_dynamic-update-slice_fusion
  437.8 6.6 %select_add_fusion = f32[512,2048]{1,0:T(8,128)} fusion(f32[512,2048]{1,0:T(8,128)} %constant_dynamic-update-slice_fusion, f32[512,2048]{1,0:T(8,128)} %collective-permute-done.2, pred[]{:T(512)S(6)} %eq.4), kind=kLoop, calls=%fused_computation.5 | loop fusion | flops 2097152 | bytes 12582913 | tf_op jit(solution)/shard_map/add | solution.py:38
  444.4 12.9 %all-gather.10.cloned.1.call-done = f32[2048,128]{1,0:T(8,128)} async-done(((f32[512,128]{1,0:T(8,128)}), f32[2048,128]{1,0:T(8,128)}) %all-gather.10.cloned.1.call-update) | async-done | bytes 1048592 | tf_op jit(solution)/shard_map/all_gather | solution.py:86
  457.3 5.5 multiply_reduce_fusion.4
  462.8 7.7 %all-reduce = (f32[128]{0:T(128)S(1)}, f32[128]{0:T(128)S(1)}) all-reduce(f32[128]{0:T(128)S(1)} %get-tuple-element.9, f32[128]{0:T(128)S(1)} %get-tuple-element.8), channel_id=1, replica_groups=mesh['x'=4,'z'=4,'c'=2,'feat'=4] {'feat'}, use_global_device_ids=true, to_apply=%region_5.6 | all-reduce | flops 256 | bytes 2048 | tf_op jit(solution)/shard_map/psum | solution.py:77
  470.6 0.1 multiply_reduce_fusion.3
  470.7 6.0 psum.44
  476.7 0.7 multiply_add_fusion.1
  477.4 0.0 all-gather.14.cloned.1.call-start
  477.5 27.6 %all-gather.12.cloned.1.call-done = f32[2048,128]{1,0:T(8,128)} async-done(((f32[512,128]{1,0:T(8,128)}), f32[2048,128]{1,0:T(8,128)}) %all-gather.12.cloned.1.call-update) | async-done | bytes 1048592 | tf_op jit(solution)/shard_map/all_gather | solution.py:86
  505.1 5.9 multiply_reduce_fusion.2
  511.1 7.7 %psum.45 = f32[128]{0:T(128)S(1)} all-reduce(f32[128]{0:T(128)S(1)} %get-tuple-element.19), channel_id=1, replica_groups=mesh['x'=4,'z'=4,'c'=2,'feat'=4] {'feat'}, use_global_device_ids=true, to_apply=%region_14.15 | all-reduce | flops 128 | bytes 1024 | tf_op jit(solution)/shard_map/psum | solution.py:77
  518.8 0.1 multiply_reduce_fusion.1
  518.9 6.2 %psum.46 = f32[128]{0:T(128)S(1)} all-reduce(f32[128]{0:T(128)S(1)} %multiply_reduce_fusion.1), channel_id=1, replica_groups=mesh['x'=4,'z'=4,'c'=2,'feat'=4] {'feat'}, use_global_device_ids=true, to_apply=%region_16.17 | all-reduce | flops 128 | bytes 1024 | tf_op jit(solution)/shard_map/psum | solution.py:77
  525.1 0.8 multiply_add_fusion
  525.9 27.7 %all-gather.14.cloned.1.call-done = f32[2048,128]{1,0:T(8,128)} async-done(((f32[512,128]{1,0:T(8,128)}), f32[2048,128]{1,0:T(8,128)}) %all-gather.14.cloned.1.call-update) | async-done | bytes 1048592 | tf_op jit(solution)/shard_map/all_gather | solution.py:86
  553.6 6.1 fusion.8
  559.7 7.7 %psum.47 = f32[128]{0:T(128)S(1)} all-reduce(f32[128]{0:T(128)S(1)} %fusion.8), channel_id=1, replica_groups=mesh['x'=4,'z'=4,'c'=2,'feat'=4] {'feat'}, use_global_device_ids=true, to_apply=%region_18.19 | all-reduce | flops 128 | bytes 1024 | tf_op jit(solution)/shard_map/psum | solution.py:77
  567.4 1.0 add_convert_fusion
  568.4 10.5 %all_gather.51 = bf16[2048,128]{1,0:T(8,128)(2,1)S(1)} all-gather(bf16[512,128]{1,0:T(8,128)(2,1)S(1)} %add_convert_fusion), channel_id=1, replica_groups=mesh['x'=4,'z'=4,'c'=2,'feat'=4] {'feat'}, dimensions={0}, use_global_device_ids=true | all-gather | bytes 655360 | tf_op jit(solution)/shard_map/all_gather | solution.py:99
  578.9 2.6 convolution_convert_fusion
  581.6 22.1 %all_to_all.21 = bf16[32,20,128]{2,1,0:T(8,128)(2,1)S(1)} all-to-all(bf16[32,20,128]{2,1,0:T(8,128)(2,1)S(1)} %reshape.59), channel_id=1, replica_groups=mesh['x'=4,'z'=4,'c'=2,'feat'=4] {'x','z','c'}, dimensions={0} | all-to-all | bytes 327680 | tf_op jit(solution)/shard_map/all_to_all | solution.py:101
  603.8 4.3 scatter_custom_fusion
  608.1 0.2 multiply_reduce_fusion
  608.2 0.6 broadcast_multiply_fusion
  (40 shorter events, 0.4 us)
Async XLA Ops:
  8.0 5.3 copy-start
  77.2 5.3 copy-start.3
  82.5 122.3 %all-to-all-start.1 = ((bf16[4,640,2048]{2,1,0:T(8,128)(2,1)}), bf16[4,640,2048]{2,1,0:T(8,128)(2,1)}, u32[]{:S(2)}, u32[]{:S(2)}) async-start(bf16[4,640,2048]{2,1,0:T(8,128)(2,1)} %stack.3), calls=%async_computation.1 | async-start | bytes 20971520 | tf_op jit(solution)/shard_map/all_to_all | solution.py:61
  88.5 217.6 %all-gather.16.cloned.1.call-start = ((), (), s32[]{:S(2)}) async-start(), calls=%async_computation.7 | async-start | bytes 10485760 | tf_op jit(solution)/shard_map/all_gather | solution.py:28
  215.2 8.1 %collective-permute-start.2 = (f32[512,2048]{1,0:T(8,128)}, f32[512,2048]{1,0:T(8,128)}, u32[]{:S(2)}, u32[]{:S(2)}) collective-permute-start(f32[512,2048]{1,0:T(8,128)} %fusion), channel_id=1, source_target_pairs={{0,4},{4,0},{1,5},{5,1},{2,6},{6,2},{3,7},{7,3},{8,12},{12,8},{9,1... | collective-permute-start | bytes 12582920 | tf_op jit(solution)/shard_map/ppermute | solution.py:24
  227.2 169.4 %all-gather.18.cloned.1.call-start = ((), (), s32[]{:S(2)}) async-start(), calls=%async_computation.8 | async-start | bytes 10485760 | tf_op jit(solution)/shard_map/all_gather | solution.py:31
  306.1 6.6 %copy-start.2 = (bf16[640,128]{1,0:T(8,128)(2,1)S(1)}, bf16[640,128]{1,0:T(8,128)(2,1)}, u32[]{:S(2)}) copy-start(bf16[640,128]{1,0:T(8,128)(2,1)} %param.4) | copy-start | bytes 491524
  315.6 15.7 %all-to-all-start.2 = ((bf16[32,20,128]{2,1,0:T(8,128)(2,1)}), bf16[32,20,128]{2,1,0:T(8,128)(2,1)S(1)}, u32[]{:S(2)}, u32[]{:S(2)}) async-start(bf16[32,20,128]{2,1,0:T(8,128)(2,1)} %broadcast_select_fusion.1), calls=%async_computation.2 | async-start | bytes 393216 | tf_op jit(solution)/shard_map/all_to_all | solution.py:55
  323.0 134.3 %all-gather.10.cloned.1.call-start = ((), (), s32[]{:S(2)}) async-start(), calls=%async_computation.4 | async-start | bytes 1310720 | tf_op jit(solution)/shard_map/all_gather | solution.py:86
  345.8 61.4 %collective-permute-start = (f32[512,128]{1,0:T(8,128)S(1)}, f32[512,128]{1,0:T(8,128)S(1)}, u32[]{:S(2)}, u32[]{:S(2)}) collective-permute-start(f32[512,128]{1,0:T(8,128)S(1)} %fusion.2), channel_id=1, source_target_pairs={{0,4},{4,0},{1,5},{5,1},{2,6},{6,2},{3,7},{7,3},{8,12},{12,8},{9,1... | collective-permute-start | bytes 786440 | tf_op jit(solution)/shard_map/ppermute | solution.py:24
  406.4 29.8 %collective-permute-start.3 = (f32[256,2048]{1,0:T(8,128)}, f32[256,2048]{1,0:T(8,128)S(1)}, u32[]{:S(2)}, u32[]{:S(2)}) collective-permute-start(f32[256,2048]{1,0:T(8,128)} %get-tuple-element.15), channel_id=1, source_target_pairs={{0,4},{4,0},{1,5},{5,1},{2,6},{6,2},{3,7},{7,3},{8,12},{12,8},{9,1... | collective-permute-start | bytes 6291464 | tf_op jit(solution)/shard_map/ppermute | solution.py:34
  429.1 6.3 %collective-permute-start.1 = (f32[256,128]{1,0:T(8,128)S(1)}, f32[256,128]{1,0:T(8,128)S(1)}, u32[]{:S(2)}, u32[]{:S(2)}) collective-permute-start(f32[256,128]{1,0:T(8,128)S(1)} %get-tuple-element.17), channel_id=1, source_target_pairs={{0,4},{4,0},{1,5},{5,1},{2,6},{6,2},{3,7},{7,3},{8,12},{12,8},{9,1... | collective-permute-start | bytes 393224 | tf_op jit(solution)/shard_map/ppermute | solution.py:34
  436.1 69.0 %all-gather.12.cloned.1.call-start = ((), (), s32[]{:S(2)}) async-start(), calls=%async_computation.5 | async-start | bytes 1310720 | tf_op jit(solution)/shard_map/all_gather | solution.py:86
  437.8 19.5 %copy-start.4 = (f32[512,128]{1,0:T(8,128)S(1)}, f32[512,128]{1,0:T(8,128)}, u32[]{:S(2)}) copy-start(f32[512,128]{1,0:T(8,128)} %add_multiply_fusion) | copy-start | bytes 786436
  477.4 47.7 %copy-start.5 = (f32[512,128]{1,0:T(8,128)S(1)}, f32[512,128]{1,0:T(8,128)}, u32[]{:S(2)}) copy-start(f32[512,128]{1,0:T(8,128)} %multiply_add_fusion.1) | copy-start | bytes 786436
  477.4 76.1 %all-gather.14.cloned.1.call-start = ((), (), s32[]{:S(2)}) async-start(), calls=%async_computation.6 | async-start | bytes 1310720 | tf_op jit(solution)/shard_map/all_gather | solution.py:86
  553.6 55.3 %copy-start.1 = (bf16[640,2048]{1,0:T(8,128)(2,1)S(1)}, bf16[640,2048]{1,0:T(8,128)(2,1)}, u32[]{:S(2)}) copy-start(bf16[640,2048]{1,0:T(8,128)(2,1)} %param.3) | copy-start | bytes 7864324
  608.0 0.8 copy-start.6
Sparse Core Ops, SparseCore 0:
  227.4 78.7 all-gather.15
  312.8 83.8 all-gather.17
Sparse Core Ops, SparseCore 1:
  436.2 21.0 all-gather.9
  477.5 27.5 all-gather.11
  526.0 27.5 all-gather.13
